TPU v7x, 512 devices: a whole 4x8x8 slice. The times are simulated.
512 devices in a mesh: group: 8 (over z_lo, core), dp: 8 (over y), tensor: 8 (over z_hi, x).
Axes of the slice: x: 4, y: 8, z: 8 (z_hi: 2, z_lo: 4; z = z_hi * 4 + z_lo), core: 2. Of those that a mesh axis runs over, the one named last changes fastest.
Arguments:
- keyvalue_local: float32 [8, 2, 4096, 1024], P('group', None, 'dp', 'tensor'), may hold values from -6 to 6
- keyvalue_anchor: float32 [2, 4096, 1024], P(None, 'dp', 'tensor'), may hold values from -6 to 6
- keyvalue_state: float32 [2, 4096, 1024], P(None, 'dp', 'tensor'), may hold values from -6 to 6
- router_local: float32 [8, 4096, 8], P('group', 'dp'), may hold values from -6 to 6
- router_anchor: float32 [4096, 8], P('dp'), may hold values from -6 to 6
- router_state: float32 [4096, 8], P('dp'), may hold values from -6 to 6
- gain_local: float32 [8, 2, 4096], P('group', None, 'dp'), may hold values from -6 to 6
- gain_anchor: float32 [2, 4096], P(None, 'dp'), may hold values from -6 to 6
- gain_state: float32 [2, 4096], P(None, 'dp'), may hold values from -6 to 6
- embed_local: float32 [8, 1000, 4096], P('group', 'dp', 'tensor'), may hold values from -6 to 6
- embed_anchor: float32 [1000, 4096], P('dp', 'tensor'), may hold values from -6 to 6
- embed_state: float32 [1000, 4096], P('dp', 'tensor'), may hold values from -6 to 6
- embed_basis: float32 [4096, 64], P('tensor'), may hold values from -0.25 to 0.25
- outer_rate: float32 [], replicated, may hold values from 0.5 to 1
Outputs:
- keyvalue_average: float32 [2, 4096, 1024], P(None, 'dp', 'tensor')
- keyvalue_momentum: float32 [2, 4096, 1024], P(None, 'dp', 'tensor')
- keyvalue_updated: float32 [2, 4096, 1024], P(None, 'dp', 'tensor')
- router_average: float32 [4096, 8], P('dp')
- router_momentum: float32 [4096, 8], P('dp')
- router_updated: float32 [4096, 8], P('dp')
- gain_average: float32 [2, 4096], P(None, 'dp')
- gain_momentum: float32 [2, 4096], P(None, 'dp')
- gain_updated: float32 [2, 4096], P(None, 'dp')
- embed_average: float32 [1000, 4096], P('dp', 'tensor')
- embed_momentum: float32 [1000, 4096], P('dp', 'tensor')
- embed_updated: float32 [1000, 4096], P('dp', 'tensor')
All inputs are finite; a program needn't handle non-finite values.
Results may differ from a plain program's by a relative error of at most 0.0001.
Values sent between devices are 32-bit elements; how exact they have to be, the bound alone decides.
No kernel may reach another device: no remote copies, remote signals or barrier semaphores. Data moves between devices by JAX's collectives and lax.ppermute only.
A program may use at most 64 MiB of HBM per device.

v0:
```python
import jax
import jax.numpy as jnp
from jax import lax
from jax.sharding import PartitionSpec as P


def nesterov(average, state, anchor, outer_rate):
    momentum = 0.5 * state + average
    updated = anchor - outer_rate * (average + 0.5 * momentum)
    return (average, momentum, updated)


def owned_slice(whole, position, count, axis_dim):
    return lax.dynamic_slice_in_dim(whole, position * count, count, axis_dim)


def local(
    keyvalue_local,
    keyvalue_anchor,
    keyvalue_state,
    router_local,
    router_anchor,
    router_state,
    gain_local,
    gain_anchor,
    gain_state,
    embed_local,
    embed_anchor,
    embed_state,
    embed_basis,
    outer_rate,
):
    groups = lax.axis_size("group")
    keyvalue_diff = keyvalue_anchor - keyvalue_local[0]
    router_diff = router_anchor - router_local[0]
    gain_diff = gain_anchor - gain_local[0]
    keyvalue_sum, router_sum, gain_sum = (
        lax.psum_scatter(keyvalue_diff, "group", scatter_dimension=1, tiled=True),
        lax.psum_scatter(router_diff, "group", scatter_dimension=0, tiled=True),
        lax.psum_scatter(gain_diff, "group", scatter_dimension=1, tiled=True),
    )
    position = lax.axis_index("group")
    keyvalue_rows = keyvalue_anchor.shape[1] // groups
    router_rows = router_anchor.shape[0] // groups
    gain_rows = gain_anchor.shape[1] // groups
    keyvalue_part = nesterov(
        keyvalue_sum / groups,
        owned_slice(keyvalue_state, position, keyvalue_rows, 1),
        owned_slice(keyvalue_anchor, position, keyvalue_rows, 1),
        outer_rate,
    )
    router_part = nesterov(
        router_sum / groups,
        owned_slice(router_state, position, router_rows, 0),
        owned_slice(router_anchor, position, router_rows, 0),
        outer_rate,
    )
    gain_part = nesterov(
        gain_sum / groups,
        owned_slice(gain_state, position, gain_rows, 1),
        owned_slice(gain_anchor, position, gain_rows, 1),
        outer_rate,
    )
    gathered = (
        lax.all_gather(keyvalue_part[0], "group", axis=1, tiled=True),
        lax.all_gather(keyvalue_part[1], "group", axis=1, tiled=True),
        lax.all_gather(keyvalue_part[2], "group", axis=1, tiled=True),
        lax.all_gather(router_part[0], "group", axis=0, tiled=True),
        lax.all_gather(router_part[1], "group", axis=0, tiled=True),
        lax.all_gather(router_part[2], "group", axis=0, tiled=True),
        lax.all_gather(gain_part[0], "group", axis=1, tiled=True),
        lax.all_gather(gain_part[1], "group", axis=1, tiled=True),
        lax.all_gather(gain_part[2], "group", axis=1, tiled=True),
    )
    keyvalue_out = gathered[0:3]
    router_out = gathered[3:6]
    gain_out = gathered[6:9]
    partial_factors = jnp.dot(
        embed_anchor - embed_local[0],
        embed_basis,
        precision=lax.Precision.HIGHEST,
        preferred_element_type=jnp.float32,
    )
    factors = lax.psum(partial_factors, ("group", "tensor"))
    factors = factors / groups
    embed_average = jnp.dot(
        factors, embed_basis.T, precision=lax.Precision.HIGHEST, preferred_element_type=jnp.float32
    )
    embed_out = nesterov(embed_average, embed_state, embed_anchor, outer_rate)
    return (
        keyvalue_out[0],
        keyvalue_out[1],
        keyvalue_out[2],
        router_out[0],
        router_out[1],
        router_out[2],
        gain_out[0],
        gain_out[1],
        gain_out[2],
        embed_out[0],
        embed_out[1],
        embed_out[2],
    )


def solution(mesh):
    in_specs = (
        P("group", None, "dp", "tensor"),
        P(None, "dp", "tensor"),
        P(None, "dp", "tensor"),
        P("group", "dp", None),
        P("dp", None),
        P("dp", None),
        P("group", None, "dp"),
        P(None, "dp"),
        P(None, "dp"),
        P("group", "dp", "tensor"),
        P("dp", "tensor"),
        P("dp", "tensor"),
        P("tensor", None),
        P(),
    )
    out_specs = (
        P(None, "dp", "tensor"),
        P(None, "dp", "tensor"),
        P(None, "dp", "tensor"),
        P("dp", None),
        P("dp", None),
        P("dp", None),
        P(None, "dp"),
        P(None, "dp"),
        P(None, "dp"),
        P("dp", "tensor"),
        P("dp", "tensor"),
        P("dp", "tensor"),
    )
    return jax.shard_map(local, mesh=mesh, in_specs=in_specs, out_specs=out_specs, check_vma=False)
```

profile of v0, /device:TPU:63, one launch (start us, length us, event | category | flops | bytes accessed | tf_op | source)
XLA Modules:
  0.0 511.7 jit_solution(6677557871619569564)
XLA Ops:
  7.2 0.0 copy-start
  7.2 0.0 reduce-scatter.12.cloned.1.call-start
  7.2 0.0 copy-start.6
  7.2 0.0 copy-start.7
  7.3 0.7 bitcast_subtract_fusion.4
  8.0 0.0 copy-start.2
  8.0 0.0 copy-start.3
  8.0 0.9 copy.46
  8.9 0.0 reduce-scatter.12.cloned.1.call-update
  8.9 0.0 reduce-scatter.10.cloned.1.call-start
  8.9 0.0 copy-done.6
  8.9 0.0 copy-done.7
  9.0 0.8 copy.44
  9.8 0.0 reduce-scatter.10.cloned.1.call-update
  9.8 0.0 reduce-scatter.8.cloned.1.call-start
  9.9 0.0 copy-done.2
  9.9 0.0 copy-done.3
  9.9 0.8 bitcast_subtract_fusion
  10.8 0.0 copy-start.1
  10.8 0.0 copy-start.4
  10.8 0.0 reduce-scatter.8.cloned.1.call-update
  11.5 0.0 copy-done
  11.5 0.2 copy-done.1
  11.7 0.1 copy-done.4
  11.8 0.0 copy-start.5
  11.8 0.4 fusion
  12.2 342.6 %psum.7 = f32[125,64]{0,1:T(8,128)S(1)} all-reduce(f32[125,64]{0,1:T(8,128)S(1)} %fusion), channel_id=1, replica_groups=mesh['group'=8,'dp'=8,'tensor'=8] {'group','tensor'}, use_global_device_ids=true, to_apply=%region_3.0 | all-reduce | flops 8000 | bytes 64000 | tf_op jit(solution)/shard_map/psum | solution.py:84
  354.8 0.0 copy-done.5
  354.8 1.3 multiply_subtract_fusion
  356.1 0.0 reduce-scatter.12.cloned.1.call-done
  356.1 0.8 copy.47
  356.9 0.8 fusion.9
  357.7 32.8 %all-gather.5 = f32[8,64,2]{1,2,0:T(2,128)S(1)} all-gather(f32[1,64,2]{1,2,0:T(2,128)S(1)} %get-tuple-element.19), channel_id=1, replica_groups=mesh['group'=8,'dp'=8,'tensor'=8] {'group'}, dimensions={0}, use_global_device_ids=true | all-gather | bytes 4608 | tf_op jit(solution)/shard_map/all_gather | solution.py:73
  390.5 0.7 reshape.35
  391.2 8.7 %all-gather.4 = f32[8,64,2]{1,2,0:T(2,128)S(1)} all-gather(f32[1,64,2]{1,2,0:T(2,128)S(1)} %get-tuple-element.20), channel_id=1, replica_groups=mesh['group'=8,'dp'=8,'tensor'=8] {'group'}, dimensions={0}, use_global_device_ids=true | all-gather | bytes 4608 | tf_op jit(solution)/shard_map/all_gather | solution.py:72
  399.9 0.7 reshape.33
  400.6 10.1 %all-gather.3 = f32[8,64,2]{1,2,0:T(2,128)S(1)} all-gather(f32[1,64,2]{1,2,0:T(2,128)S(1)} %get-tuple-element.22), channel_id=1, replica_groups=mesh['group'=8,'dp'=8,'tensor'=8] {'group'}, dimensions={0}, use_global_device_ids=true | all-gather | bytes 4608 | tf_op jit(solution)/shard_map/all_gather | solution.py:71
  410.6 0.7 reshape.31
  411.3 0.0 reduce-scatter.10.cloned.1.call-done
  411.3 0.8 copy.45
  412.1 0.8 subtract_bitcast_fusion
  412.9 14.1 %all-gather.2 = f32[8,64,8]{1,2,0:T(8,128)S(1)} all-gather(f32[1,64,8]{1,2,0:T(8,128)S(1)} %get-tuple-element.17), channel_id=1, replica_groups=mesh['group'=8,'dp'=8,'tensor'=8] {'group'}, dimensions={0}, use_global_device_ids=true | all-gather | bytes 18432 | tf_op jit(solution)/shard_map/all_gather | solution.py:70
  427.0 0.7 reshape.29
  427.7 14.1 %all-gather.1 = f32[8,64,8]{1,2,0:T(8,128)S(1)} all-gather(f32[1,64,8]{1,2,0:T(8,128)S(1)} %get-tuple-element.18), channel_id=1, replica_groups=mesh['group'=8,'dp'=8,'tensor'=8] {'group'}, dimensions={0}, use_global_device_ids=true | all-gather | bytes 18432 | tf_op jit(solution)/shard_map/all_gather | solution.py:69
  441.7 0.7 reshape.27
  442.4 14.1 %all-gather = f32[8,64,8]{1,2,0:T(8,128)S(1)} all-gather(f32[1,64,8]{1,2,0:T(8,128)S(1)} %get-tuple-element.21), channel_id=1, replica_groups=mesh['group'=8,'dp'=8,'tensor'=8] {'group'}, dimensions={0}, use_global_device_ids=true | all-gather | bytes 18432 | tf_op jit(solution)/shard_map/all_gather | solution.py:68
  456.5 0.7 reshape.25
  457.2 0.0 reduce-scatter.8.cloned.1.call-done
  457.2 0.9 multiply_subtract_fusion.1
  458.1 14.9 %all_gather.29 = f32[2,512,128]{2,1,0:T(8,128)S(1)} all-gather(f32[2,64,128]{2,1,0:T(8,128)S(1)} %get-tuple-element.14), channel_id=1, replica_groups=mesh['group'=8,'dp'=8,'tensor'=8] {'group'}, dimensions={1}, use_global_device_ids=true | all-gather | bytes 589824 | tf_op jit(solution)/shard_map/all_gather | solution.py:67
  473.0 14.9 %all_gather.28 = f32[2,512,128]{2,1,0:T(8,128)S(1)} all-gather(f32[2,64,128]{2,1,0:T(8,128)S(1)} %get-tuple-element.15), channel_id=1, replica_groups=mesh['group'=8,'dp'=8,'tensor'=8] {'group'}, dimensions={1}, use_global_device_ids=true | all-gather | bytes 589824 | tf_op jit(solution)/shard_map/all_gather | solution.py:66
  487.9 14.9 %all_gather.27 = f32[2,512,128]{2,1,0:T(8,128)S(1)} all-gather(f32[2,64,128]{2,1,0:T(8,128)S(1)} %get-tuple-element.16), channel_id=1, replica_groups=mesh['group'=8,'dp'=8,'tensor'=8] {'group'}, dimensions={1}, use_global_device_ids=true | all-gather | bytes 589824 | tf_op jit(solution)/shard_map/all_gather | solution.py:65
  502.8 0.8 copy.57
  503.6 0.8 copy.58
  504.4 0.8 copy.59
  (7 shorter events, 0.0 us)
Async XLA Ops:
  7.2 4.3 copy-start
  7.2 348.9 %reduce-scatter.12.cloned.1.call-start = ((), (), s32[]{:S(2)}) async-start(), calls=%async_computation.5 | async-start | bytes 294912
  7.2 1.7 copy-start.6
  7.2 1.7 copy-start.7
  8.0 1.9 copy-start.2
  8.0 1.9 copy-start.3
  8.9 402.4 %reduce-scatter.10.cloned.1.call-start = ((), (), s32[]{:S(2)}) async-start(), calls=%async_computation.4 | async-start | bytes 294912
  9.8 447.4 %reduce-scatter.8.cloned.1.call-start = ((), (), s32[]{:S(2)}) async-start(), calls=%async_computation.3 | async-start | bytes 589824 | tf_op jit(solution)/shard_map/reduce_scatter | solution.py:38
  10.8 0.9 copy-start.1
  10.8 1.0 copy-start.4
  11.8 343.0 %copy-start.5 = (f32[125,512]{1,0:T(8,128)S(1)}, f32[125,512]{1,0:T(8,128)}, u32[]{:S(2)}) copy-start(f32[125,512]{1,0:T(8,128)} %param.25) | copy-start | bytes 768004
Sparse Core Ops, SparseCore 0:
  11.4 40.1 reduce-scatter.11
  54.9 37.6 reduce-scatter.9
  96.0 38.3 reduce-scatter.7
where the time goes:
time: 512 us
  blocking collectives  481 us (94%)
  between operations  14.6 us (3%)
  local copies, waits for them, and re-layouts  10.1 us (2%)
    psum x1, blocking collectives, local(): factors = lax.psum(partial_factors, ('group', 'tensor'))  343 us
    all_gather x1, blocking collectives, local(): lax.all_gather(gain_part[2], 'group', axis=1, tiled=True)  32.8 us
    all_gather x1, blocking collectives, local(): lax.all_gather(keyvalue_part[2], 'group', axis=1, tiled=True)  14.9 us
    all_gather x1, blocking collectives, local(): lax.all_gather(keyvalue_part[1], 'group', axis=1, tiled=True)  14.9 us
    all_gather x1, blocking collectives, local(): lax.all_gather(keyvalue_part[0], 'group', axis=1, tiled=True)  14.9 us
    all_gather x1, blocking collectives, local(): lax.all_gather(router_part[2], 'group', axis=0, tiled=True)  14.1 us
    all_gather x1, blocking collectives, local(): lax.all_gather(router_part[0], 'group', axis=0, tiled=True)  14.1 us
    all_gather x1, blocking collectives, local(): lax.all_gather(router_part[1], 'group', axis=0, tiled=True)  14.1 us
  transfers between devices with their start and end apart: 3, of which 0 were waited for; matrix products, arithmetic and copies ran while one was open for 2% of the time, Pallas kernels for 0%

commit v1 on v0

--- a/solution.py
+++ b/solution.py
@@ -2,6 +2,12 @@
 import jax.numpy as jnp
 from jax import lax
 from jax.sharding import PartitionSpec as P
+
+
+def add_all(x, axis):
+    parts = lax.all_gather(x, axis, axis=0, tiled=False)
+    total = parts.sum(axis=0)
+    return total
 
 
 def nesterov(average, state, anchor, outer_rate):
@@ -81,7 +87,7 @@
         precision=lax.Precision.HIGHEST,
         preferred_element_type=jnp.float32,
     )
-    factors = lax.psum(partial_factors, ("group", "tensor"))
+    factors = add_all(partial_factors, ("group", "tensor"))
     factors = factors / groups
     embed_average = jnp.dot(
         factors, embed_basis.T, precision=lax.Precision.HIGHEST, preferred_element_type=jnp.float32

time: 512 us -> 227 us (0.44)
  the two profiles are of different devices: /device:TPU:63 before, /device:TPU:128 now
where the time goes in v1:
time: 227 us; the launch traced here: 226 us
  blocking collectives  122 us (54%)
  waiting for transfers between devices  67.8 us (30%)
  between operations  15.9 us (7%)
  local copies, waits for them, and re-layouts  9.82 us (4%)
  other arithmetic  7.87 us (3%)
  matrix products  2.35 us (1%)
    unnamed x6, waiting for transfers between devices  40.2 us
    all_gather x1, waiting for transfers between devices, add_all(): parts = lax.all_gather(x, axis, axis=0, tiled=False)  27.6 us
    all_gather x1, blocking collectives, local(): lax.all_gather(router_part[2], 'group', axis=0, tiled=True)  18.1 us
    all_gather x1, blocking collectives, local(): lax.all_gather(keyvalue_part[1], 'group', axis=1, tiled=True)  15.3 us
    all_gather x1, blocking collectives, local(): lax.all_gather(keyvalue_part[0], 'group', axis=1, tiled=True)  15.2 us
    all_gather x1, blocking collectives, local(): lax.all_gather(keyvalue_part[2], 'group', axis=1, tiled=True)  15 us
    all_gather x1, blocking collectives, local(): lax.all_gather(router_part[0], 'group', axis=0, tiled=True)  14.1 us
    all_gather x1, blocking collectives, local(): lax.all_gather(router_part[1], 'group', axis=0, tiled=True)  14.1 us
  transfers between devices with their start and end apart: 4, of which 3 were waited for; matrix products, arithmetic and copies ran while one was open for 6% of the time, Pallas kernels for 0%

profile of v1, /device:TPU:128, one launch (start us, length us, event | category | flops | bytes accessed | tf_op | source)
XLA Modules:
  0.0 226.4 jit_solution(5394918467994137667)
XLA Ops:
  8.0 0.0 copy-start
  8.0 0.0 copy-start.1
  8.0 0.0 copy-start.2
  8.0 0.0 reduce-scatter.12.cloned.1.call-start
  8.1 0.8 bitcast_subtract_fusion.4
  8.9 0.9 copy.46
  9.7 0.0 reduce-scatter.12.cloned.1.call-update
  9.7 0.0 reduce-scatter.10.cloned.1.call-start
  9.8 0.7 bitcast_subtract_fusion.3
  10.5 0.8 copy.44
  11.4 0.0 reduce-scatter.10.cloned.1.call-update
  11.4 0.0 reduce-scatter.8.cloned.1.call-start
  11.5 2.0 bitcast_subtract_fusion
  13.5 0.0 reduce-scatter.8.cloned.1.call-update
  13.5 0.0 all-gather.10.cloned.1.call-start
  13.6 0.0 copy-done
  13.6 0.0 copy-done.1
  13.6 0.0 copy-done.2
  13.6 1.0 convolution_bitcast_fusion
  14.6 0.0 all-gather.10.cloned.1.call-update
  15.3 33.2 %reduce-scatter.12.cloned.1.call-done = f32[64,2]{1,0:T(8,128)} async-done(((f32[512,2]{1,0:T(8,128)}), f32[64,2]{1,0:T(8,128)}) %reduce-scatter.12.cloned.1.call-update) | async-done | bytes 528
  48.5 0.8 copy.47
  49.3 0.8 fusion.8
  50.1 11.9 %all-gather.6 = f32[8,64,2]{1,2,0:T(2,128)S(1)} all-gather(f32[1,64,2]{1,2,0:T(2,128)S(1)} %get-tuple-element.19), channel_id=1, replica_groups=mesh['group'=8,'dp'=8,'tensor'=8] {'group'}, dimensions={0}, use_global_device_ids=true | all-gather | bytes 4608 | tf_op jit(solution)/shard_map/all_gather | solution.py:79
  61.9 0.7 reshape.36
  62.6 10.1 %all-gather.5 = f32[8,64,2]{1,2,0:T(2,128)S(1)} all-gather(f32[1,64,2]{1,2,0:T(2,128)S(1)} %get-tuple-element.20), channel_id=1, replica_groups=mesh['group'=8,'dp'=8,'tensor'=8] {'group'}, dimensions={0}, use_global_device_ids=true | all-gather | bytes 4608 | tf_op jit(solution)/shard_map/all_gather | solution.py:78
  72.7 0.7 reshape.34
  73.3 8.8 %all-gather.4 = f32[8,64,2]{1,2,0:T(2,128)S(1)} all-gather(f32[1,64,2]{1,2,0:T(2,128)S(1)} %get-tuple-element.22), channel_id=1, replica_groups=mesh['group'=8,'dp'=8,'tensor'=8] {'group'}, dimensions={0}, use_global_device_ids=true | all-gather | bytes 4608 | tf_op jit(solution)/shard_map/all_gather | solution.py:77
  82.1 0.7 reshape.32
  82.8 7.0 %reduce-scatter.10.cloned.1.call-done = f32[64,8]{1,0:T(8,128)} async-done(((f32[512,8]{1,0:T(8,128)}), f32[64,8]{1,0:T(8,128)}) %reduce-scatter.10.cloned.1.call-update) | async-done | bytes 2064
  89.8 0.8 copy.45
  90.6 0.8 subtract_bitcast_fusion
  91.4 18.1 %all-gather.3 = f32[8,64,8]{1,2,0:T(8,128)S(1)} all-gather(f32[1,64,8]{1,2,0:T(8,128)S(1)} %get-tuple-element.17), channel_id=1, replica_groups=mesh['group'=8,'dp'=8,'tensor'=8] {'group'}, dimensions={0}, use_global_device_ids=true | all-gather | bytes 18432 | tf_op jit(solution)/shard_map/all_gather | solution.py:76
  109.5 0.7 reshape.30
  110.2 14.1 %all-gather.2 = f32[8,64,8]{1,2,0:T(8,128)S(1)} all-gather(f32[1,64,8]{1,2,0:T(8,128)S(1)} %get-tuple-element.18), channel_id=1, replica_groups=mesh['group'=8,'dp'=8,'tensor'=8] {'group'}, dimensions={0}, use_global_device_ids=true | all-gather | bytes 18432 | tf_op jit(solution)/shard_map/all_gather | solution.py:75
  124.3 0.7 reshape.28
  125.0 14.1 %all-gather.1 = f32[8,64,8]{1,2,0:T(8,128)S(1)} all-gather(f32[1,64,8]{1,2,0:T(8,128)S(1)} %get-tuple-element.21), channel_id=1, replica_groups=mesh['group'=8,'dp'=8,'tensor'=8] {'group'}, dimensions={0}, use_global_device_ids=true | all-gather | bytes 18432 | tf_op jit(solution)/shard_map/all_gather | solution.py:74
  139.0 0.7 reshape.26
  139.7 0.0 copy-start.3
  139.7 0.0 reduce-scatter.8.cloned.1.call-done
  139.7 1.0 multiply_subtract_fusion.1
  140.7 15.0 %all_gather.35 = f32[2,512,128]{2,1,0:T(8,128)S(1)} all-gather(f32[2,64,128]{2,1,0:T(8,128)S(1)} %get-tuple-element.14), channel_id=1, replica_groups=mesh['group'=8,'dp'=8,'tensor'=8] {'group'}, dimensions={1}, use_global_device_ids=true | all-gather | bytes 589824 | tf_op jit(solution)/shard_map/all_gather | solution.py:73
  155.7 15.3 %all_gather.34 = f32[2,512,128]{2,1,0:T(8,128)S(1)} all-gather(f32[2,64,128]{2,1,0:T(8,128)S(1)} %get-tuple-element.15), channel_id=1, replica_groups=mesh['group'=8,'dp'=8,'tensor'=8] {'group'}, dimensions={1}, use_global_device_ids=true | all-gather | bytes 589824 | tf_op jit(solution)/shard_map/all_gather | solution.py:72
  171.0 15.2 %all_gather.33 = f32[2,512,128]{2,1,0:T(8,128)S(1)} all-gather(f32[2,64,128]{2,1,0:T(8,128)S(1)} %get-tuple-element.16), channel_id=1, replica_groups=mesh['group'=8,'dp'=8,'tensor'=8] {'group'}, dimensions={1}, use_global_device_ids=true | all-gather | bytes 589824 | tf_op jit(solution)/shard_map/all_gather | solution.py:71
  186.2 27.6 %all-gather.10.cloned.1.call-done = f32[64,125,64]{1,2,0:T(8,128)} async-done(((f32[1,125,64]{1,2,0:T(8,128)}), f32[64,125,64]{1,2,0:T(8,128)}) %all-gather.10.cloned.1.call-update) | async-done | bytes 2048016 | tf_op jit(solution)/shard_map/all_gather | solution.py:8
  213.8 1.8 reduce_sum.9
  215.6 0.0 copy-done.3
  215.6 1.3 multiply_subtract_fusion
  216.9 0.8 copy.57
  217.7 0.8 copy.58
  218.5 0.8 copy.59
  (6 shorter events, 0.0 us)
Async XLA Ops:
  8.0 5.6 %copy-start = (f32[512,64]{0,1:T(8,128)S(1)}, f32[512,64]{0,1:T(8,128)}, u32[]{:S(2)}) copy-start(f32[512,64]{0,1:T(8,128)} %param.26) | copy-start | bytes 393220
  8.0 5.6 %copy-start.1 = (f32[125,512]{1,0:T(8,128)S(1)}, f32[125,512]{1,0:T(8,128)}, u32[]{:S(2)}) copy-start(f32[125,512]{1,0:T(8,128)} %param.24) | copy-start | bytes 768004
  8.0 5.6 %copy-start.2 = (f32[1,125,512]{2,0,1:T(1,128)S(1)}, f32[1,125,512]{2,0,1:T(1,128)}, u32[]{:S(2)}) copy-start(f32[1,125,512]{2,0,1:T(1,128)} %param.23) | copy-start | bytes 768004
  8.0 40.4 %reduce-scatter.12.cloned.1.call-start = ((), (), s32[]{:S(2)}) async-start(), calls=%async_computation.6 | async-start | bytes 294912
  9.7 80.0 %reduce-scatter.10.cloned.1.call-start = ((), (), s32[]{:S(2)}) async-start(), calls=%async_computation.5 | async-start | bytes 294912
  11.4 128.3 %reduce-scatter.8.cloned.1.call-start = ((), (), s32[]{:S(2)}) async-start(), calls=%async_computation.3 | async-start | bytes 589824 | tf_op jit(solution)/shard_map/reduce_scatter | solution.py:44
  13.5 200.3 %all-gather.10.cloned.1.call-start = ((), (), s32[]{:S(2)}) async-start(), calls=%async_computation.4 | async-start | bytes 2129920 | tf_op jit(solution)/shard_map/all_gather | solution.py:8
  139.7 75.8 %copy-start.3 = (f32[125,512]{1,0:T(8,128)S(1)}, f32[125,512]{1,0:T(8,128)}, u32[]{:S(2)}) copy-start(f32[125,512]{1,0:T(8,128)} %param.25) | copy-start | bytes 768004
Sparse Core Ops, SparseCore 0:
  12.2 36.1 reduce-scatter.11
  51.8 37.9 reduce-scatter.9
  93.1 38.0 reduce-scatter.7
Sparse Core Ops, SparseCore 1:
  16.7 197.0 all-gather.9
